TPU v7x, 32 devices: a whole 2x2x4 slice. The times are simulated.
32 devices in a mesh: ctx: 16 (over z, y, x), head: 2 (over core).
Axes of the slice: x: 2, y: 2, z: 4, core: 2. Of those that a mesh axis runs over, the one named last changes fastest.
Arguments:
- queries: bfloat16 [2048, 4096], P('ctx', 'head'), may hold values from -48 to 48
- keys: bfloat16 [2048, 2048], P('ctx', 'head'), may hold values from -6 to 6
- values: bfloat16 [2048, 2048], P('ctx', 'head'), may hold values from -6 to 6
- hidden_in: bfloat16 [2048, 4608], P('ctx', 'head'), may hold values from -6 to 6
- out_weight: bfloat16 [4096, 4608], P('ctx', 'head'), may hold values from -0.09375 to 0.09375
- out_gain: float32 [4608], P('head'), may hold values from 0.1 to 1.9
- reward_weight: float32 [4608], P('head'), may hold values from -0.09375 to 0.09375
- doc_lengths: int32 [16], replicated, may hold values from 1 to 1024, 2048 in all
Outputs:
- hidden_out: bfloat16 [2048, 4608], P('ctx', 'head')
- rewards: float32 [16], replicated
Inputs may be any that keep to these rules, and one draw needn't show every extreme that they name: `doc_lengths`: the lengths sum to 2048; the longest is exactly 1024.
All inputs are finite; a program needn't handle non-finite values.
Results may differ from a plain program's by a relative error of at most 0.005.
Values may be sent and summed in bfloat16 or wider, within the bound.
No kernel may reach another device: no remote copies, remote signals or barrier semaphores. Data moves between devices by JAX's collectives and lax.ppermute only.
A program may use at most 128 MiB of HBM per device.

v0:
```python
import jax
import jax.numpy as jnp
from jax import lax
from jax.sharding import Mesh, PartitionSpec as P

D = 4608
QUERY_HEADS = 32
KEY_VALUE_HEADS = 16
HEAD_WIDTH = 128
NDOC = 16
soft_cap = 50.0
CTX = ("ca", "cb")


def storage_positions(rows, tok_dev, n_ctx):
    owner = rows // tok_dev
    offset = rows % tok_dev
    half = tok_dev // 2
    slab = jnp.where(offset < half, owner, 2 * n_ctx - 1 - owner)
    return slab * half + offset % half


def document_of(positions, doc_ends):
    return jnp.sum((positions[:, None] >= doc_ends[None, :]).astype(jnp.int32), axis=1)


def shards(queries, keys, values, hidden_in, out_weight, out_gain, reward_weight, doc_lengths):
    n_ctx = lax.axis_size(CTX)
    device = lax.axis_index(CTX)
    tok_dev = queries.shape[0]
    kv_local = keys.shape[1] // HEAD_WIDTH
    group_repeat = QUERY_HEADS // KEY_VALUE_HEADS
    scale = (D / QUERY_HEADS) ** (-0.5)
    doc_ends = jnp.cumsum(doc_lengths)
    local_rows = device * tok_dev + jnp.arange(tok_dev, dtype=jnp.int32)
    query_pos = storage_positions(local_rows, tok_dev, n_ctx)
    query_doc = document_of(query_pos, doc_ends)
    q_groups = queries.reshape(tok_dev, kv_local, group_repeat, HEAD_WIDTH)
    span = tok_dev * max(1, 2048 // tok_dev)

    def attend_block(state, key_piece, value_piece, start):
        count = key_piece.shape[0]
        key_rows = start + jnp.arange(count, dtype=jnp.int32)
        key_pos = storage_positions(key_rows, tok_dev, n_ctx)
        key_doc = document_of(key_pos, doc_ends)
        visible = (query_doc[:, None] == key_doc[None, :]) & (
            key_pos[None, :] <= query_pos[:, None]
        )

        def compute(carry):
            numerator, denominator = carry
            scores = (
                jnp.einsum(
                    "qgrd,kgd->grqk",
                    q_groups,
                    key_piece.reshape(count, kv_local, HEAD_WIDTH),
                    preferred_element_type=jnp.float32,
                )
                * scale
            )
            scores = soft_cap * jnp.tanh(scores / soft_cap)
            weights = jnp.where(visible[None, None], jnp.exp(scores), 0.0)
            numerator = numerator + jnp.einsum(
                "grqk,kgd->grqd",
                weights.astype(jnp.bfloat16),
                value_piece.reshape(count, kv_local, HEAD_WIDTH),
                preferred_element_type=jnp.float32,
            )
            denominator = denominator + jnp.sum(weights, axis=-1)
            return (numerator, denominator)

        return lax.cond(jnp.any(visible), compute, lambda carry: carry, state)

    def attend(state, key_piece, value_piece, start):
        count = key_piece.shape[0]
        if count <= span:
            return attend_block(state, key_piece, value_piece, start)
        blocks = count // span
        whole = blocks * span
        width = key_piece.shape[1]
        key_blocks = key_piece[:whole].reshape(blocks, span, width)
        value_blocks = value_piece[:whole].reshape(blocks, span, width)
        starts = start + span * jnp.arange(blocks, dtype=jnp.int32)

        def step_fn(carry, item):
            return (attend_block(carry, item[0], item[1], item[2]), None)

        state, _ = lax.scan(step_fn, state, (key_blocks, value_blocks, starts))
        if whole < count:
            state = attend_block(state, key_piece[whole:], value_piece[whole:], start + whole)
        return state

    initial = (
        jnp.zeros((kv_local, group_repeat, tok_dev, HEAD_WIDTH), jnp.float32),
        jnp.zeros((kv_local, group_repeat, tok_dev), jnp.float32),
    )
    kv_width = keys.shape[1]
    both = lax.all_gather(jnp.concatenate([keys, values], axis=1), CTX, axis=0, tiled=True)
    numerator, denominator = attend(initial, both[:, :kv_width], both[:, kv_width:], jnp.int32(0))
    attended = (numerator / denominator[..., None]).astype(jnp.bfloat16)
    attended = attended.transpose(2, 0, 1, 3).reshape(tok_dev, kv_local * group_repeat * HEAD_WIDTH)
    all_heads = lax.all_gather(attended, "head", axis=1, tiled=True)
    weight_rows = lax.all_gather(out_weight, "cb", axis=0, tiled=True)
    regrouped = lax.all_to_all(all_heads, "ca", 1, 0, tiled=True)
    partial = jnp.dot(regrouped, weight_rows, preferred_element_type=jnp.float32)
    mixed = lax.psum_scatter(partial, "ca", scatter_dimension=0, tiled=True)
    squares = lax.psum(jnp.sum(mixed * mixed, axis=1), "head")
    normed = mixed / jnp.sqrt(squares / D + 1e-06)[:, None]
    out32 = hidden_in.astype(jnp.float32) + normed * out_gain[None, :]
    tok_reward = jnp.sum(out32 * reward_weight[None, :], axis=1)
    onehot = (query_doc[:, None] == jnp.arange(NDOC, dtype=jnp.int32)[None, :]).astype(jnp.float32)
    partial_sums = jnp.sum(onehot * tok_reward[:, None], axis=0)
    totals = lax.psum(partial_sums, CTX + ("head",))
    rewards = totals / jnp.sqrt(doc_lengths.astype(jnp.float32))
    return (out32.astype(jnp.bfloat16), rewards)


def solution(mesh):
    n_ctx, n_head = mesh.devices.shape
    inner = 1
    while inner * inner * 4 <= n_ctx:
        inner *= 2
    split = Mesh(mesh.devices.reshape(n_ctx // inner, inner, n_head), ("ca", "cb", "head"))
    rows = P(CTX, "head")
    in_specs = (rows, rows, rows, rows, rows, P("head"), P("head"), P())
    out_specs = (rows, P())
    return jax.shard_map(
        shards, mesh=split, in_specs=in_specs, out_specs=out_specs, check_vma=False
    )
```

profile of v0, /device:TPU:0, one launch (start us, length us, event | category | flops | bytes accessed | tf_op | source)
XLA Modules:
  0.0 398.0 jit_solution(5263270378748125020)
XLA Ops:
  7.2 0.0 all-gather.4.cloned.1.call-start
  7.2 1.1 copy.28
  8.3 1.1 copy.29
  9.5 0.8 pad_maximum_fusion
  10.3 0.0 all-gather.4.cloned.1.call-update
  10.3 0.0 all-gather.6.cloned.1.call-start
  10.4 0.7 copy.27
  11.1 0.1 reduce
  11.3 0.1 convert_reduce_fusion.1
  11.4 0.1 convert_reduce_fusion
  11.5 1.9 fusion.24
  14.0 142.4 %all-gather.4.cloned.1.call-done = bf16[2048,2048]{0,1:T(8,128)(2,1)} async-done(((bf16[128,2048]{0,1:T(8,128)(2,1)}), bf16[2048,2048]{0,1:T(8,128)(2,1)}) %all-gather.4.cloned.1.call-update) | async-done | bytes 8388624 | tf_op jit(solution)/shard_map/all_gather | solution.py:98
  156.4 26.9 %conditional.1 = (f32[8,2,128]{2,1,0:T(2,128)S(1)}, f32[8,2,128,128]{2,3,1,0:T(8,128)S(1)}) conditional(s32[]{:T(128)} %convert_element_type.28, () %tuple.16, (pred[128,2048]{0,1:T(8,128)(4,1)S(1)}, bf16[2048,2048]{0,1:T(8,128)(2,1)}, bf16[128,2048]{1,0:T(8,128)(2,1)}) %tuple.17), branch_computations={%region_4.5_spmd, %region_5.7_spmd} | conditional | flops 2181036032 | bytes 80748616 | solution.py:72
  156.4 0.0 copy-start.2
  156.4 6.1 %fusion.25 = (bf16[2048,1024]{0,1:T(8,128)(2,1)}, bf16[2048,1024]{0,1:T(8,128)(2,1)}) fusion(bf16[2048,2048]{0,1:T(8,128)(2,1)} %get-tuple-element.11), kind=kLoop, calls=%fused_computation.55 | loop fusion | bytes 16777216 | tf_op jit(solution)/shard_map/slice | solution.py:99
  162.4 0.0 copy-done.2
  162.4 0.4 reshape.165
  162.8 0.0 copy-start
  162.8 11.8 %fusion = (f32[8,2,128]{2,1,0:T(2,128)S(1)}, f32[8,2048,128,2]{2,1,3,0:T(8,128)}) fusion(pred[128,2048]{0,1:T(8,128)(4,1)S(1)} %get-tuple-element.10, bf16[2048,8,128,1]{0,2,3,1:T(8,128)(2,1)} %bitcast.30, bf16[128,8,2,128]{3,2,1,0:T(2,128)(2,1)S(1)} %reshape.165), kind=kOutput, calls=%fused_computation.1 | convolution fusion | flops 1090516992 | bytes 21766144 | tf_op jit(solution)/shard_map/cond/branch_1_fun/qgrd,kgd->grqk/dot_general | solution.py:53
  174.6 0.0 copy-done
  174.6 8.6 %fusion.2 = f32[8,2,128,128]{2,3,1,0:T(8,128)S(1)} fusion(bf16[2048,8,128,1]{0,2,3,1:T(8,128)(2,1)S(1)} %bitcast.29, f32[8,2048,128,2]{2,1,3,0:T(8,128)} %get-tuple-element.27, pred[128,2048]{0,1:T(8,128)(4,1)S(1)} %get-tuple-element.10), kind=kOutput, calls=%fused_computation.3 | convolution fusion | flops 1090519040 | bytes 22282240 | tf_op jit(solution)/shard_map/cond | solution.py:72
  183.2 0.9 divide_convert_fusion
  184.2 0.0 all-gather.6.cloned.1.call-update
  184.2 0.0 all-gather.8.cloned.1.call-start
  184.2 0.7 all-gather.8.cloned.1.call-update
  184.9 6.6 %all-gather.6.cloned.1.call-done = bf16[128,4096]{0,1:T(8,128)(2,1)} async-done(((bf16[128,2048]{0,1:T(8,128)(2,1)}), bf16[128,4096]{0,1:T(8,128)(2,1)}) %all-gather.6.cloned.1.call-update) | async-done | bytes 1048592 | tf_op jit(solution)/shard_map/all_gather | solution.py:102
  191.6 2.3 copy.31
  193.9 4.9 %all-to-all-start = ((bf16[128,4,1024]{2,0,1:T(8,128)(2,1)}), bf16[128,4,1024]{2,0,1:T(8,128)(2,1)S(1)}, u32[]{:S(2)}, u32[]{:S(2)}) async-start(bf16[128,4,1024]{2,0,1:T(8,128)(2,1)} %copy.31), calls=%async_computation | async-start | bytes 2097152 | tf_op jit(solution)/shard_map/all_to_all | solution.py:104
  198.7 0.0 reduce-scatter.2.cloned.1.call-start
  198.7 53.0 %all-gather.8.cloned.1.call-done = bf16[1024,2304]{1,0:T(8,128)(2,1)} async-done(((bf16[256,2304]{1,0:T(8,128)(2,1)}), bf16[1024,2304]{1,0:T(8,128)(2,1)}) %all-gather.8.cloned.1.call-update) | async-done | bytes 4718608 | tf_op jit(solution)/shard_map/all_gather | solution.py:103
  251.7 0.0 all-to-all-done
  251.7 6.6 %fusion.26 = f32[512,2304]{1,0:T(8,128)} fusion(bf16[512,1024]{1,0:T(8,128)(2,1)S(1)} %bitcast.33, bf16[1024,2304]{1,0:T(8,128)(2,1)} %all-gather.8.cloned.1.call-done), kind=kOutput, calls=%fused_computation.56 | convolution fusion | flops 2415919104 | bytes 10485760 | tf_op jit(solution)/shard_map/dot_general | solution.py:105
  258.3 0.0 copy-start.1
  258.3 0.0 copy-start.3
  258.3 0.0 copy-start.4
  258.3 0.0 copy-start.5
  258.3 0.0 reduce-scatter.2.cloned.1.call-update
  258.3 85.4 %reduce-scatter.2.cloned.1.call-done = f32[128,2304]{1,0:T(8,128)} async-done(((f32[512,2304]{1,0:T(8,128)}), f32[128,2304]{1,0:T(8,128)}) %reduce-scatter.2.cloned.1.call-update) | async-done | bytes 1179664 | tf_op jit(solution)/shard_map/reduce_scatter | solution.py:106
  343.7 1.4 multiply_reduce_fusion.1
  345.2 2.5 psum.14
  347.6 0.0 copy-done.1
  347.6 0.0 copy-done.3
  347.7 0.0 copy-done.4
  347.7 2.4 multiply_reduce_fusion
  350.1 0.1 select_reduce_fusion
  350.2 40.8 %psum.15 = f32[16]{0:T(128)S(1)} all-reduce(f32[16]{0:T(128)S(1)} %select_reduce_fusion), channel_id=1, replica_groups=mesh['ca'=4,'cb'=4,'head'=2] {'ca','cb','head'}, use_global_device_ids=true, to_apply=%region_12.13 | all-reduce | flops 16 | bytes 128 | tf_op jit(solution)/shard_map/psum | solution.py:113
  391.0 0.0 copy-done.5
  391.0 0.5 rsqrt_multiply_fusion
  (4 shorter events, 0.1 us)
Async XLA Ops:
  7.2 149.2 %all-gather.4.cloned.1.call-start = ((), (), s32[]{:S(2)}) async-start(), calls=%async_computation.2 | async-start | bytes 8912896 | tf_op jit(solution)/shard_map/all_gather | solution.py:98
  10.3 181.3 %all-gather.6.cloned.1.call-start = ((), (), s32[]{:S(2)}) async-start(), calls=%async_computation.3 | async-start | bytes 1572864 | tf_op jit(solution)/shard_map/all_gather | solution.py:102
  156.4 6.1 %copy-start.2 = (bf16[128,2048]{1,0:T(8,128)(2,1)S(1)}, bf16[128,2048]{1,0:T(8,128)(2,1)}, u32[]{:S(2)}) copy-start(bf16[128,2048]{1,0:T(8,128)(2,1)} %get-tuple-element.20) | copy-start | bytes 1572868 | tf_op jit(solution)/shard_map/cond
  162.8 11.8 %copy-start = (bf16[2048,1024]{0,1:T(8,128)(2,1)S(1)}, bf16[2048,1024]{0,1:T(8,128)(2,1)}, u32[]{:S(2)}) copy-start(bf16[2048,1024]{0,1:T(8,128)(2,1)} %get-tuple-element.24) | copy-start | bytes 12582916 | tf_op jit(solution)/shard_map/cond
  184.2 67.5 %all-gather.8.cloned.1.call-start = ((), (), s32[]{:S(2)}) async-start(), calls=%async_computation.4 | async-start | bytes 5898240 | tf_op jit(solution)/shard_map/all_gather | solution.py:103
  193.9 57.8 %all-to-all-start = ((bf16[128,4,1024]{2,0,1:T(8,128)(2,1)}), bf16[128,4,1024]{2,0,1:T(8,128)(2,1)S(1)}, u32[]{:S(2)}, u32[]{:S(2)}) async-start(bf16[128,4,1024]{2,0,1:T(8,128)(2,1)} %copy.31), calls=%async_computation | async-start | bytes 2097152 | tf_op jit(solution)/shard_map/all_to_all | solution.py:104
  198.7 145.0 %reduce-scatter.2.cloned.1.call-start = ((), (), s32[]{:S(2)}) async-start(), calls=%async_computation.5 | async-start | bytes 5898240 | tf_op jit(solution)/shard_map/reduce_scatter | solution.py:106
  258.3 89.3 %copy-start.1 = (bf16[128,2304]{1,0:T(8,128)(2,1)S(1)}, bf16[128,2304]{1,0:T(8,128)(2,1)}, u32[]{:S(2)}) copy-start(bf16[128,2304]{1,0:T(8,128)(2,1)} %param.13) | copy-start | bytes 1769476
  258.3 89.4 %copy-start.3 = (f32[2304]{0:T(1024)S(1)}, f32[2304]{0:T(1024)}, u32[]{:S(2)}) copy-start(f32[2304]{0:T(1024)} %param.16) | copy-start | bytes 27652
  258.3 89.4 %copy-start.4 = (f32[2304]{0:T(1024)S(1)}, f32[2304]{0:T(1024)}, u32[]{:S(2)}) copy-start(f32[2304]{0:T(1024)} %param.15) | copy-start | bytes 27652
  258.3 132.7 %copy-start.5 = (s32[16]{0:T(128)S(1)}, s32[16]{0:T(128)}, u32[]{:S(2)}) copy-start(s32[16]{0:T(128)} %param.17) | copy-start | bytes 196
Sparse Core Ops, SparseCore 0:
  11.3 145.0 all-gather.3
  184.3 7.2 all-gather.5
  193.4 58.2 all-gather.7
  258.5 85.2 reduce-scatter.1
where the time goes:
time: 399 us; the launch traced here: 398 us
  waiting for transfers between devices  288 us (72%)
  blocking collectives  43.2 us (11%)
  matrix products  27 us (7%)
  between operations  14.5 us (4%)
  local copies, waits for them, and re-layouts  11.7 us (3%)
  other arithmetic  8.5 us (2%)
  starting transfers between devices  4.98 us (1%)
    all_gather x1, waiting for transfers between devices, shards(): lax.all_gather(jnp.concatenate([keys, values], axis=1), CTX, axis=0, tile...  142 us
    reduce_scatter x1, waiting for transfers between devices, shards(): mixed = lax.psum_scatter(partial, 'ca', scatter_dimension=0, tiled=True)  85.4 us
    all_gather x1, waiting for transfers between devices, shards(): weight_rows = lax.all_gather(out_weight, 'cb', axis=0, tiled=True)  53 us
    psum x1, blocking collectives, shards(): totals = lax.psum(partial_sums, CTX + ('head',))  40.8 us
    dot_general x1, matrix products, compute(): jnp.einsum('qgrd,kgd->grqk', q_groups, key_piece.reshape(count, kv_local,...  11.8 us
    cond x1, matrix products, attend_block(): return lax.cond(jnp.any(visible), compute, lambda carry: carry, state)  8.62 us
  transfers between devices with their start and end apart: 5, of which 4 were waited for; matrix products, arithmetic and copies ran while one was open for 1% of the time, Pallas kernels for 0%

commit v1 on v0

--- a/solution.py
+++ b/solution.py
@@ -110,7 +110,7 @@
     tok_reward = jnp.sum(out32 * reward_weight[None, :], axis=1)
     onehot = (query_doc[:, None] == jnp.arange(NDOC, dtype=jnp.int32)[None, :]).astype(jnp.float32)
     partial_sums = jnp.sum(onehot * tok_reward[:, None], axis=0)
-    totals = lax.psum(partial_sums, CTX + ("head",))
+    totals = jnp.sum(lax.all_gather(partial_sums, CTX + ("head",)), axis=0)
     rewards = totals / jnp.sqrt(doc_lengths.astype(jnp.float32))
     return (out32.astype(jnp.bfloat16), rewards)
 

time: 399 us -> 399 us (level)
    psum x1 -> x0, blocking collectives: 40.8 us -> none  [shards(): totals = lax.psum(partial_sums, CTX + ('head',))]
    unnamed x0 -> x1, blocking collectives: none -> 40.7 us
where the time goes in v1:
time: 399 us; the launch traced here: 398 us
  waiting for transfers between devices  288 us (72%)
  blocking collectives  43.2 us (11%)
  matrix products  27 us (7%)
  between operations  14.5 us (4%)
  local copies, waits for them, and re-layouts  12 us (3%)
  other arithmetic  8.53 us (2%)
  starting transfers between devices  4.98 us (1%)
    all_gather x1, waiting for transfers between devices, shards(): lax.all_gather(jnp.concatenate([keys, values], axis=1), CTX, axis=0, tile...  142 us
    reduce_scatter x1, waiting for transfers between devices, shards(): mixed = lax.psum_scatter(partial, 'ca', scatter_dimension=0, tiled=True)  85.4 us
    all_gather x1, waiting for transfers between devices, shards(): weight_rows = lax.all_gather(out_weight, 'cb', axis=0, tiled=True)  53 us
    unnamed x1, blocking collectives  40.7 us
    dot_general x1, matrix products, compute(): jnp.einsum('qgrd,kgd->grqk', q_groups, key_piece.reshape(count, kv_local,...  11.8 us
    cond x1, matrix products, attend_block(): return lax.cond(jnp.any(visible), compute, lambda carry: carry, state)  8.61 us
  transfers between devices with their start and end apart: 5, of which 4 were waited for; matrix products, arithmetic and copies ran while one was open for 1% of the time, Pallas kernels for 0%

profile of v1, /device:TPU:0, one launch (start us, length us, event | category | flops | bytes accessed | tf_op | source)
XLA Modules:
  0.0 398.4 jit_solution(5564755888755323602)
XLA Ops:
  7.2 0.0 all-gather.5.cloned.1.call-start
  7.2 1.1 copy.28
  8.3 1.1 copy.29
  9.5 0.8 pad_maximum_fusion
  10.3 0.0 all-gather.5.cloned.1.call-update
  10.3 0.0 all-gather.7.cloned.1.call-start
  10.4 0.7 copy.27
  11.1 0.1 reduce
  11.3 0.1 convert_reduce_fusion.1
  11.4 0.1 convert_reduce_fusion
  11.5 1.9 fusion.24
  14.0 142.3 %all-gather.5.cloned.1.call-done = bf16[2048,2048]{0,1:T(8,128)(2,1)} async-done(((bf16[128,2048]{0,1:T(8,128)(2,1)}), bf16[2048,2048]{0,1:T(8,128)(2,1)}) %all-gather.5.cloned.1.call-update) | async-done | bytes 8388624 | tf_op jit(solution)/shard_map/all_gather | solution.py:98
  156.4 26.9 %conditional.1 = (f32[8,2,128]{2,1,0:T(2,128)S(1)}, f32[8,2,128,128]{2,3,1,0:T(8,128)S(1)}) conditional(s32[]{:T(128)} %convert_element_type.28, () %tuple.16, (pred[128,2048]{0,1:T(8,128)(4,1)S(1)}, bf16[2048,2048]{0,1:T(8,128)(2,1)}, bf16[128,2048]{1,0:T(8,128)(2,1)}) %tuple.17), branch_computations={%region_4.5_spmd, %region_5.7_spmd} | conditional | flops 2181036032 | bytes 80748616 | solution.py:72
  156.4 0.0 copy-start.2
  156.4 6.1 %fusion.25 = (bf16[2048,1024]{0,1:T(8,128)(2,1)}, bf16[2048,1024]{0,1:T(8,128)(2,1)}) fusion(bf16[2048,2048]{0,1:T(8,128)(2,1)} %get-tuple-element.11), kind=kLoop, calls=%fused_computation.55 | loop fusion | bytes 16777216 | tf_op jit(solution)/shard_map/slice | solution.py:99
  162.4 0.0 copy-done.2
  162.4 0.4 reshape.165
  162.8 0.0 copy-start
  162.8 11.8 %fusion = (f32[8,2,128]{2,1,0:T(2,128)S(1)}, f32[8,2048,128,2]{2,1,3,0:T(8,128)}) fusion(pred[128,2048]{0,1:T(8,128)(4,1)S(1)} %get-tuple-element.10, bf16[2048,8,128,1]{0,2,3,1:T(8,128)(2,1)} %bitcast.30, bf16[128,8,2,128]{3,2,1,0:T(2,128)(2,1)S(1)} %reshape.165), kind=kOutput, calls=%fused_computation.1 | convolution fusion | flops 1090516992 | bytes 21766144 | tf_op jit(solution)/shard_map/cond/branch_1_fun/qgrd,kgd->grqk/dot_general | solution.py:53
  174.6 0.0 copy-done
  174.6 8.6 %fusion.2 = f32[8,2,128,128]{2,3,1,0:T(8,128)S(1)} fusion(bf16[2048,8,128,1]{0,2,3,1:T(8,128)(2,1)S(1)} %bitcast.29, f32[8,2048,128,2]{2,1,3,0:T(8,128)} %get-tuple-element.27, pred[128,2048]{0,1:T(8,128)(4,1)S(1)} %get-tuple-element.10), kind=kOutput, calls=%fused_computation.3 | convolution fusion | flops 1090519040 | bytes 22282240 | tf_op jit(solution)/shard_map/cond | solution.py:72
  183.2 0.9 divide_convert_fusion
  184.2 0.0 all-gather.7.cloned.1.call-update
  184.2 0.0 all-gather.9.cloned.1.call-start
  184.2 0.7 all-gather.9.cloned.1.call-update
  184.9 6.6 %all-gather.7.cloned.1.call-done = bf16[128,4096]{0,1:T(8,128)(2,1)} async-done(((bf16[128,2048]{0,1:T(8,128)(2,1)}), bf16[128,4096]{0,1:T(8,128)(2,1)}) %all-gather.7.cloned.1.call-update) | async-done | bytes 1048592 | tf_op jit(solution)/shard_map/all_gather | solution.py:102
  191.6 2.3 copy.31
  193.9 4.9 %all-to-all-start = ((bf16[128,4,1024]{2,0,1:T(8,128)(2,1)}), bf16[128,4,1024]{2,0,1:T(8,128)(2,1)S(1)}, u32[]{:S(2)}, u32[]{:S(2)}) async-start(bf16[128,4,1024]{2,0,1:T(8,128)(2,1)} %copy.31), calls=%async_computation | async-start | bytes 2097152 | tf_op jit(solution)/shard_map/all_to_all | solution.py:104
  198.7 0.0 reduce-scatter.2.cloned.1.call-start
  198.7 53.0 %all-gather.9.cloned.1.call-done = bf16[1024,2304]{1,0:T(8,128)(2,1)} async-done(((bf16[256,2304]{1,0:T(8,128)(2,1)}), bf16[1024,2304]{1,0:T(8,128)(2,1)}) %all-gather.9.cloned.1.call-update) | async-done | bytes 4718608 | tf_op jit(solution)/shard_map/all_gather | solution.py:103
  251.7 0.0 all-to-all-done
  251.7 6.6 %fusion.26 = f32[512,2304]{1,0:T(8,128)} fusion(bf16[512,1024]{1,0:T(8,128)(2,1)S(1)} %bitcast.33, bf16[1024,2304]{1,0:T(8,128)(2,1)} %all-gather.9.cloned.1.call-done), kind=kOutput, calls=%fused_computation.56 | convolution fusion | flops 2415919104 | bytes 10485760 | tf_op jit(solution)/shard_map/dot_general | solution.py:105
  258.3 0.0 copy-start.1
  258.3 0.0 copy-start.3
  258.3 0.0 reduce-scatter.2.cloned.1.call-update
  258.3 85.4 %reduce-scatter.2.cloned.1.call-done = f32[128,2304]{1,0:T(8,128)} async-done(((f32[512,2304]{1,0:T(8,128)}), f32[128,2304]{1,0:T(8,128)}) %reduce-scatter.2.cloned.1.call-update) | async-done | bytes 1179664 | tf_op jit(solution)/shard_map/reduce_scatter | solution.py:106
  343.8 1.4 multiply_reduce_fusion.1
  345.2 2.5 psum.7
  347.7 0.0 copy-done.1
  347.7 0.0 copy-done.3
  347.7 0.0 copy-done.4
  347.7 2.4 multiply_reduce_fusion
  350.1 0.1 select_reduce_fusion
  350.2 0.2 dynamic-update-slice
  350.5 40.7 %all-reduce = f32[512]{0:T(512)S(1)} all-reduce(f32[512]{0:T(512)S(1)} %dynamic-update-slice), channel_id=2, replica_groups=mesh['ca'=4,'cb'=4,'head'=2] {'ca','cb','head'}, use_global_device_ids=true, to_apply=%add | all-reduce | flops 512 | bytes 4096
  391.2 0.1 reshape.173
  391.3 0.0 copy-done.5
  391.3 0.5 rsqrt_multiply_fusion
  (8 shorter events, 0.1 us)
Async XLA Ops:
  7.2 149.2 %all-gather.5.cloned.1.call-start = ((), (), s32[]{:S(2)}) async-start(), calls=%async_computation.2 | async-start | bytes 8912896 | tf_op jit(solution)/shard_map/all_gather | solution.py:98
  10.3 181.3 %all-gather.7.cloned.1.call-start = ((), (), s32[]{:S(2)}) async-start(), calls=%async_computation.3 | async-start | bytes 1572864 | tf_op jit(solution)/shard_map/all_gather | solution.py:102
  156.4 6.1 %copy-start.2 = (bf16[128,2048]{1,0:T(8,128)(2,1)S(1)}, bf16[128,2048]{1,0:T(8,128)(2,1)}, u32[]{:S(2)}) copy-start(bf16[128,2048]{1,0:T(8,128)(2,1)} %get-tuple-element.20) | copy-start | bytes 1572868 | tf_op jit(solution)/shard_map/cond
  162.8 11.8 %copy-start = (bf16[2048,1024]{0,1:T(8,128)(2,1)S(1)}, bf16[2048,1024]{0,1:T(8,128)(2,1)}, u32[]{:S(2)}) copy-start(bf16[2048,1024]{0,1:T(8,128)(2,1)} %get-tuple-element.24) | copy-start | bytes 12582916 | tf_op jit(solution)/shard_map/cond
  184.2 67.5 %all-gather.9.cloned.1.call-start = ((), (), s32[]{:S(2)}) async-start(), calls=%async_computation.4 | async-start | bytes 5898240 | tf_op jit(solution)/shard_map/all_gather | solution.py:103
  193.9 57.8 %all-to-all-start = ((bf16[128,4,1024]{2,0,1:T(8,128)(2,1)}), bf16[128,4,1024]{2,0,1:T(8,128)(2,1)S(1)}, u32[]{:S(2)}, u32[]{:S(2)}) async-start(bf16[128,4,1024]{2,0,1:T(8,128)(2,1)} %copy.31), calls=%async_computation | async-start | bytes 2097152 | tf_op jit(solution)/shard_map/all_to_all | solution.py:104
  198.7 145.0 %reduce-scatter.2.cloned.1.call-start = ((), (), s32[]{:S(2)}) async-start(), calls=%async_computation.5 | async-start | bytes 5898240 | tf_op jit(solution)/shard_map/reduce_scatter | solution.py:106
  258.3 89.4 %copy-start.1 = (bf16[128,2304]{1,0:T(8,128)(2,1)S(1)}, bf16[128,2304]{1,0:T(8,128)(2,1)}, u32[]{:S(2)}) copy-start(bf16[128,2304]{1,0:T(8,128)(2,1)} %param.13) | copy-start | bytes 1769476
  258.3 89.4 %copy-start.3 = (f32[2304]{0:T(1024)S(1)}, f32[2304]{0:T(1024)}, u32[]{:S(2)}) copy-start(f32[2304]{0:T(1024)} %param.16) | copy-start | bytes 27652
  258.3 89.4 %copy-start.4 = (f32[2304]{0:T(1024)S(1)}, f32[2304]{0:T(1024)}, u32[]{:S(2)}) copy-start(f32[2304]{0:T(1024)} %param.15) | copy-start | bytes 27652
  258.3 133.0 %copy-start.5 = (s32[16]{0:T(128)S(1)}, s32[16]{0:T(128)}, u32[]{:S(2)}) copy-start(s32[16]{0:T(128)} %param.17) | copy-start | bytes 196
Sparse Core Ops, SparseCore 0:
  11.3 145.0 all-gather.4
  184.3 7.2 all-gather.6
  193.4 58.2 all-gather.8
  258.4 85.2 reduce-scatter.1
